TPU v7x, 32 devices: a whole 2x2x4 slice. The times are simulated.
32 devices in a mesh: req: 2 (over x), ctx: 8 (over z, core), exp: 2 (over y).
Axes of the slice: x: 2, y: 2, z: 4, core: 2. Of those that a mesh axis runs over, the one named last changes fastest.
Arguments:
- query_states: bfloat16 [2, 512, 1024], P('req', 'ctx', 'exp'), may hold values from -6 to 6
- key_states: bfloat16 [2, 512, 1024], P('req', 'ctx', 'exp'), may hold values from -6 to 6
- value_states: bfloat16 [2, 512, 1024], P('req', 'ctx', 'exp'), may hold values from -6 to 6
- residual: bfloat16 [2, 512, 2048], P('req', ('ctx', 'exp')), may hold values from -6 to 6
- out_weight: bfloat16 [2048, 1024], P('ctx', 'exp'), may hold values from -0.1875 to 0.1875
- norm_gain: float32 [2048], replicated, may hold values from 0.1 to 1.9
- gate_weight: bfloat16 [8, 2048, 704], P('ctx', None, 'exp'), may hold values from -0.125 to 0.125
- up_weight: bfloat16 [8, 2048, 704], P('ctx', None, 'exp'), may hold values from -0.125 to 0.125
- down_weight: bfloat16 [8, 704, 2048], P('ctx', 'exp'), may hold values from -0.21875 to 0.21875
- routes: int32 [2, 512, 4], P('req', 'ctx'), may hold values from 0 to 7, all different within a row; in each aligned block of 64 rows (0 to 63, 64 to 127, ..., all dimensions but the last counted through in order) at most 48 rows name the same one
- route_weights: float32 [2, 512, 4], P('req', 'ctx'), may hold values from 0.1 to 1
- prompt_lengths: int32 [2], P('req'), may hold values from 128 to 512, as said below
Outputs:
- layer_out: bfloat16 [2, 512, 2048], P('req', ('ctx', 'exp'))
- cache_keys: bfloat16 [2, 512, 1024], P('req', 'ctx', 'exp')
- cache_values: bfloat16 [2, 512, 1024], P('req', 'ctx', 'exp')
Inputs may be any that keep to these rules, and one draw needn't show every extreme that they name: `routes`: each row names 4 different experts; in each aligned block of 64 rows of a request no expert is named by more than 48 rows, a bound that some block reaches. `prompt_lengths`: one request has exactly 512 tokens.
All inputs are finite; a program needn't handle non-finite values.
Results may differ from a plain program's by a relative error of at most 0.019.
Values may be sent and summed in bfloat16 or wider, within the bound.
No kernel may reach another device: no remote copies, remote signals or barrier semaphores. Data moves between devices by JAX's collectives and lax.ppermute only.
A program may use at most 64 MiB of HBM per device.

v0:
```python
import jax
import jax.numpy as jnp
from jax import lax
from jax.sharding import PartitionSpec as P

D = 2048
HD = 128
TOP = 4
EPS = 1e-06
NEG = -1e30


def row_positions(row_ids, half_block, n_groups):
    block_ids = row_ids // half_block
    device = block_ids // 2
    target = jnp.where(block_ids % 2 == 0, device, 2 * n_groups - 1 - device)
    return target * half_block + row_ids % half_block


def slot_tables(route_block, weight_block, experts, capacity):
    tok_here, top_here = route_block.shape
    flat_ids = route_block.reshape(tok_here * top_here)
    hit_table = (flat_ids[:, None] == jnp.arange(experts, dtype=jnp.int32)[None, :]).astype(
        jnp.int32
    )
    before = jnp.cumsum(hit_table, axis=0) - hit_table
    slot_rank = jnp.sum(before * hit_table, axis=1)
    slot_index = flat_ids * capacity + slot_rank
    slot_match = (
        jnp.arange(experts * capacity, dtype=jnp.int32)[:, None] == slot_index[None, :]
    ).astype(jnp.float32)
    slot_match = slot_match.reshape(experts * capacity, tok_here, top_here)
    dispatch = jnp.sum(slot_match, axis=2)
    combine = jnp.transpose(jnp.sum(slot_match * weight_block[None, :, :], axis=2))
    return (dispatch, combine)


def expert_ffn(token_rows, gate_matrix, up_matrix, down_matrix):
    gate_act = jnp.dot(token_rows, gate_matrix, preferred_element_type=jnp.float32)
    up_act = jnp.dot(token_rows, up_matrix, preferred_element_type=jnp.float32)
    hidden = (jax.nn.silu(gate_act) * up_act).astype(jnp.bfloat16)
    return jnp.dot(hidden, down_matrix, preferred_element_type=jnp.float32)


def exp_swap(x):
    return lax.ppermute(x, "exp", perm=[(0, 1), (1, 0)])


def exp_reduce_rows(parts):
    if lax.axis_size("exp") != 2:
        return lax.psum_scatter(
            parts.astype(jnp.bfloat16), "exp", scatter_dimension=0, tiled=True
        ).astype(jnp.float32)
    half = parts.shape[0] // 2
    first = lax.axis_index("exp") == 0
    lower = parts[:half]
    upper = parts[half:]
    mine = jnp.where(first, lower, upper)
    theirs = jnp.where(first, upper, lower)
    got = exp_swap(theirs.astype(jnp.bfloat16))
    return mine + got.astype(jnp.float32)


def exp_gather_rows(rows):
    if lax.axis_size("exp") != 2:
        return lax.all_gather(rows, "exp", axis=0, tiled=True)
    got = exp_swap(rows)
    first = lax.axis_index("exp") == 0
    return jnp.where(
        first, jnp.concatenate([rows, got], axis=0), jnp.concatenate([got, rows], axis=0)
    )


def local(
    query_states,
    key_states,
    value_states,
    residual,
    out_weight,
    norm_gain,
    gate_weight,
    up_weight,
    down_weight,
    routes,
    route_weights,
    prompt_lengths,
):
    n_ctx = lax.axis_size("ctx")
    my_ctx = lax.axis_index("ctx")
    tok_here = query_states.shape[1]
    feat_width = query_states.shape[2]
    heads_dev = feat_width // HD
    half_block = tok_here // 2
    score_scale = HD ** (-0.5)
    length = prompt_lengths[0]
    local_ids = jnp.arange(tok_here, dtype=jnp.int32)
    query_pos = row_positions(my_ctx * tok_here + local_ids, half_block, n_ctx)
    decode_pos = my_ctx * tok_here + local_ids
    query_three = query_states[0].reshape(tok_here, heads_dev, HD)
    run_max = jnp.full((heads_dev, tok_here), NEG, jnp.float32)
    kv_here = jnp.concatenate([key_states[0], value_states[0]], axis=1)
    kv_all = lax.all_gather(kv_here, "ctx", axis=0, tiled=True)
    key_two = kv_all[:, :feat_width]
    value_two = kv_all[:, feat_width:]
    row_count = key_two.shape[0]
    key_pos = row_positions(jnp.arange(row_count, dtype=jnp.int32), half_block, n_ctx)
    pick_rows = (decode_pos[:, None] == key_pos[None, :]).astype(jnp.bfloat16)
    kept_keys = jnp.dot(pick_rows, key_two, preferred_element_type=jnp.float32)
    kept_values = jnp.dot(pick_rows, value_two, preferred_element_type=jnp.float32)
    old_max = run_max
    key_heads = key_two.reshape(row_count, heads_dev, HD)
    value_heads = value_two.reshape(row_count, heads_dev, HD)
    logits = (
        jnp.einsum("qhd,khd->hqk", query_three, key_heads, preferred_element_type=jnp.float32)
        * score_scale
    )
    visible = (key_pos[None, :] <= query_pos[:, None]) & (key_pos[None, :] < length)
    logits = jnp.where(visible[None], logits, NEG)
    new_max = jnp.maximum(old_max, jnp.max(logits, axis=2))
    weights = jnp.where(visible[None], jnp.exp(logits - new_max[:, :, None]), 0.0)
    new_sum = jnp.sum(weights, axis=2)
    gained = jnp.einsum(
        "hqk,khd->hqd",
        weights.astype(jnp.bfloat16),
        value_heads,
        preferred_element_type=jnp.float32,
    )
    inner_state = (new_max, new_sum, gained)
    run_max, run_sum, run_out, kept_keys, kept_values = inner_state + (kept_keys, kept_values)
    mixed = (run_out / run_sum[:, :, None]).astype(jnp.bfloat16)
    mixed = jnp.transpose(mixed, (1, 0, 2)).reshape(tok_here, feat_width)
    out_parts = jnp.einsum(
        "tc,oc->to",
        mixed,
        lax.all_gather(out_weight, "ctx", axis=0, tiled=True),
        preferred_element_type=jnp.float32,
    )
    head_total = exp_reduce_rows(out_parts)
    stream = (residual[0].astype(jnp.float32) + head_total).astype(jnp.bfloat16)
    stream_f = stream.astype(jnp.float32)
    mean_sq = jnp.mean(stream_f * stream_f, axis=1, keepdims=True)
    normed = (stream_f * lax.rsqrt(mean_sq + EPS) * norm_gain).astype(jnp.bfloat16)
    all_normed = exp_gather_rows(normed)
    capacity = min(tok_here, 2 * max(1, 3 * tok_here * TOP // (4 * n_ctx)))
    dispatch, combine = slot_tables(routes[0], route_weights[0], n_ctx, capacity)
    send_rows = jnp.dot(
        dispatch.astype(jnp.bfloat16), all_normed, preferred_element_type=jnp.float32
    ).astype(jnp.bfloat16)
    send_rows = send_rows.reshape(n_ctx, capacity, D)
    arrived = lax.all_to_all(send_rows, "ctx", split_axis=0, concat_axis=0, tiled=True)
    slot_count = arrived.shape[1]
    flat_rows = arrived.reshape(n_ctx * slot_count, D)
    produced = expert_ffn(flat_rows, gate_weight[0], up_weight[0], down_weight[0]).reshape(
        n_ctx, slot_count, D
    )
    served = lax.all_to_all(
        produced.astype(jnp.bfloat16), "ctx", split_axis=0, concat_axis=0, tiled=True
    ).astype(produced.dtype)
    results = served.reshape(n_ctx * capacity, D)
    moe_part = jnp.dot(
        combine, results, precision=lax.Precision.HIGHEST, preferred_element_type=jnp.float32
    )
    moe_rows = exp_reduce_rows(moe_part)
    layer_out = (stream.astype(jnp.float32) + moe_rows).astype(jnp.bfloat16)
    return (
        layer_out[None],
        kept_keys.astype(jnp.bfloat16)[None],
        kept_values.astype(jnp.bfloat16)[None],
    )


def solution(mesh):
    return jax.shard_map(
        local,
        mesh=mesh,
        in_specs=(
            P("req", "ctx", "exp"),
            P("req", "ctx", "exp"),
            P("req", "ctx", "exp"),
            P("req", ("ctx", "exp"), None),
            P("ctx", "exp"),
            P(),
            P("ctx", None, "exp"),
            P("ctx", None, "exp"),
            P("ctx", "exp", None),
            P("req", "ctx", None),
            P("req", "ctx", None),
            P("req"),
        ),
        out_specs=(P("req", ("ctx", "exp"), None), P("req", "ctx", "exp"), P("req", "ctx", "exp")),
        check_vma=False,
    )
```

profile of v0, /device:TPU:0, one launch (start us, length us, event | category | flops | bytes accessed | tf_op | source)
XLA Modules:
  0.0 180.0 jit_solution(15707757264715683724)
XLA Ops:
  7.2 0.0 copy-start
  7.2 0.0 all-gather.3.cloned.1.call-start
  7.2 1.6 pad_maximum_fusion
  8.9 0.0 all-gather.3.cloned.1.call-update
  8.9 0.0 all-gather.5.cloned.1.call-start
  8.9 0.7 all-gather.5.cloned.1.call-update
  10.3 0.8 copy.47
  11.1 0.1 eq.92
  11.2 0.6 reduce-window.6
  11.8 0.9 reshape_squeeze.4
  12.7 0.1 compare_and_fusion
  12.8 22.2 %all-gather.3.cloned.1.call-done = bf16[512,1024]{1,0:T(8,128)(2,1)} async-done(((bf16[64,1024]{1,0:T(8,128)(2,1)}), bf16[512,1024]{1,0:T(8,128)(2,1)}) %all-gather.3.cloned.1.call-update) | async-done | bytes 1048592 | tf_op jit(solution)/shard_map/all_gather | solution.py:102
  35.0 1.3 fusion.71
  36.3 0.2 copy.54
  36.5 0.2 copy.55
  36.7 0.3 fusion.72
  37.1 0.2 fusion.18
  37.3 0.3 fusion.15
  37.7 27.7 %all-gather.5.cloned.1.call-done = bf16[2048,512]{1,0:T(8,128)(2,1)} async-done(((bf16[256,512]{1,0:T(8,128)(2,1)}), bf16[2048,512]{1,0:T(8,128)(2,1)}) %all-gather.5.cloned.1.call-update) | async-done | bytes 2097168 | tf_op jit(solution)/shard_map/all_gather | solution.py:135
  65.4 2.3 %fusion.38 = f32[64,2048]{1,0:T(8,128)S(1)} fusion(bf16[2048,512]{1,0:T(8,128)(2,1)} %all-gather.5.cloned.1.call-done, bf16[4,8,8,128]{3,2,1,0:T(8,128)(2,1)S(1)} %fusion.15), kind=kOutput, calls=%fused_computation.52 | convolution fusion | flops 134217728 | bytes 2686976 | tf_op jit(solution)/shard_map/tc,oc->to/dot_general | solution.py:132
  67.7 0.0 copy-start.4
  67.8 1.5 collective-permute-start
  69.3 0.2 slice_reduce_fusion
  69.5 0.1 eq.88
  69.7 0.1 fusion.48
  69.8 0.1 reduce_sum.49
  69.9 3.6 %collective-permute-done = bf16[32,2048]{1,0:T(8,128)(2,1)S(1)} collective-permute-done((bf16[32,2048]{1,0:T(8,128)(2,1)S(1)}, bf16[32,2048]{1,0:T(8,128)(2,1)S(1)}, u32[]{:S(2)}, u32[]{:S(2)}) %collective-permute-start) | collective-permute-done | bytes 131104 | tf_op jit(solution)/shard_map/ppermute | solution.py:46
  73.5 0.2 fusion.20
  73.7 0.1 fusion.22
  73.8 1.5 collective-permute-start.1
  75.3 0.1 copy.50
  75.4 0.1 convert_reduce_fusion
  75.6 3.3 %collective-permute-done.1 = bf16[32,2048]{1,0:T(8,128)(2,1)S(1)} collective-permute-done((bf16[32,2048]{1,0:T(8,128)(2,1)S(1)}, bf16[32,2048]{1,0:T(8,128)(2,1)S(1)}, u32[]{:S(2)}, u32[]{:S(2)}) %collective-permute-start.1) | collective-permute-done | bytes 131104 | tf_op jit(solution)/shard_map/ppermute | solution.py:46
  78.8 0.6 convolution_convert_fusion.1
  79.4 41.0 %all_to_all.10 = bf16[8,48,2048]{2,1,0:T(8,128)(2,1)S(1)} all-to-all(bf16[8,48,2048]{2,1,0:T(8,128)(2,1)S(1)} %bitcast.73), channel_id=1, replica_groups=mesh['req'=2,'ctx'=8,'exp'=2] {'ctx'}, dimensions={0} | all-to-all | bytes 3145728 | tf_op jit(solution)/shard_map/all_to_all | solution.py:150
  120.4 0.9 fusion.3
  121.3 0.4 copy-done.6
  121.8 0.9 fusion.10
  122.7 0.2 copy.51
  122.9 2.1 %convolution_convert_fusion = bf16[8,48,2048]{2,1,0:T(8,128)(2,1)} fusion(bf16[8,48,352]{2,1,0:T(8,128)(2,1)S(1)} %bitcast.77, bf16[1,352,2048]{2,1,0:T(8,128)(2,1)S(1)} %copy-done), kind=kOutput, calls=%fused_computation | convolution fusion | flops 554434560 | bytes 3284992 | tf_op jit(solution)/shard_map/dot_general | solution.py:42
  125.1 3.6 %all-to-all-start.1 = ((bf16[8,48,2048]{2,1,0:T(8,128)(2,1)}), bf16[8,48,2048]{2,1,0:T(8,128)(2,1)S(1)}, u32[]{:S(2)}, u32[]{:S(2)}) async-start(bf16[8,48,2048]{2,1,0:T(8,128)(2,1)} %convolution_convert_fusion), calls=%async_computation.1 | async-start | bytes 3145728 | tf_op jit(solution)/shard_map/all_to_all | solution.py:156
  128.7 1.9 %fusion.17 = bf16[1,64,512]{2,1,0:T(8,128)(2,1)} fusion(s32[512]{0:T(512)S(1)} %fusion.56, s32[64]{0:T(128)S(1)} %iota_add_fusion, bf16[512,1024]{1,0:T(8,128)(2,1)} %all-gather.3.cloned.1.call-done), kind=kOutput, calls=%fused_computation.19 | convolution fusion | flops 33619968 | bytes 592128 | tf_op jit(solution)/shard_map/dot_general | solution.py:109
  130.6 35.8 %all-to-all-done.1 = bf16[8,48,2048]{2,1,0:T(8,128)(2,1)S(1)} async-done(((bf16[8,48,2048]{2,1,0:T(8,128)(2,1)}), bf16[8,48,2048]{2,1,0:T(8,128)(2,1)S(1)}, u32[]{:S(2)}, u32[]{:S(2)}) %all-to-all-start.1) | async-done | bytes 1572896 | tf_op jit(solution)/shard_map/all_to_all | solution.py:156
  166.4 0.9 fusion.73
  167.3 1.5 collective-permute-start.2
  168.8 0.9 fusion.16
  169.7 2.7 %collective-permute-done.2 = bf16[32,2048]{1,0:T(8,128)(2,1)S(1)} collective-permute-done((bf16[32,2048]{1,0:T(8,128)(2,1)S(1)}, bf16[32,2048]{1,0:T(8,128)(2,1)S(1)}, u32[]{:S(2)}, u32[]{:S(2)}) %collective-permute-start.2) | collective-permute-done | bytes 131104 | tf_op jit(solution)/shard_map/ppermute | solution.py:46
  172.4 0.7 fusion.37
  (23 shorter events, 0.2 us)
Async XLA Ops:
  7.2 115.8 %copy-start = (bf16[1,352,2048]{2,1,0:T(8,128)(2,1)S(1)}, bf16[1,352,2048]{2,1,0:T(8,128)(2,1)}, u32[]{:S(2)}) copy-start(bf16[1,352,2048]{2,1,0:T(8,128)(2,1)} %param.20) | copy-start | bytes 4325380
  7.2 27.9 %all-gather.3.cloned.1.call-start = ((), (), s32[]{:S(2)}) async-start(), calls=%async_computation.2 | async-start | bytes 1179648 | tf_op jit(solution)/shard_map/all_gather | solution.py:102
  8.9 56.5 %all-gather.5.cloned.1.call-start = ((), (), s32[]{:S(2)}) async-start(), calls=%async_computation.3 | async-start | bytes 2359296 | tf_op jit(solution)/shard_map/all_gather | solution.py:135
  37.7 35.8 %copy-start.2 = (bf16[1,32,2048]{2,1,0:T(8,128)(2,1)S(1)}, bf16[1,32,2048]{2,1,0:T(8,128)(2,1)}, u32[]{:S(2)}) copy-start(bf16[1,32,2048]{2,1,0:T(8,128)(2,1)} %param.15) | copy-start | bytes 393220
  37.7 36.0 %copy-start.3 = (f32[2048]{0:T(1024)S(1)}, f32[2048]{0:T(1024)}, u32[]{:S(2)}) copy-start(f32[2048]{0:T(1024)} %param.17) | copy-start | bytes 24580
  67.7 7.7 %copy-start.4 = (f32[1,64,4]{1,2,0:T(4,128)S(1)}, f32[1,64,4]{1,2,0:T(4,128)}, u32[]{:S(2)}) copy-start(f32[1,64,4]{1,2,0:T(4,128)} %param.22) | copy-start | bytes 3076
  67.8 5.7 %collective-permute-start = (bf16[32,2048]{1,0:T(8,128)(2,1)S(1)}, bf16[32,2048]{1,0:T(8,128)(2,1)S(1)}, u32[]{:S(2)}, u32[]{:S(2)}) collective-permute-start(bf16[32,2048]{1,0:T(8,128)(2,1)S(1)} %select_convert_fusion.1), channel_id=1, source_target_pairs={{0,1},{1,0},{2,3},{3,2},{4,5},{5,4},{6,7},{7,6},{8,9},{9,8},{10,11... | collective-permute-start | bytes 393224 | tf_op jit(solution)/shard_map/ppermute | solution.py:46
  73.8 5.0 %collective-permute-start.1 = (bf16[32,2048]{1,0:T(8,128)(2,1)S(1)}, bf16[32,2048]{1,0:T(8,128)(2,1)S(1)}, u32[]{:S(2)}, u32[]{:S(2)}) collective-permute-start(bf16[32,2048]{1,0:T(8,128)(2,1)S(1)} %fusion.22), channel_id=1, source_target_pairs={{0,1},{1,0},{2,3},{3,2},{4,5},{5,4},{6,7},{7,6},{8,9},{9,8},{10,11... | collective-permute-start | bytes 393224 | tf_op jit(solution)/shard_map/ppermute | solution.py:46
  79.4 41.0 %copy-start.5 = (bf16[1,2048,352]{1,2,0:T(8,128)(2,1)S(1)}, bf16[1,2048,352]{1,2,0:T(8,128)(2,1)}, u32[]{:S(2)}) copy-start(bf16[1,2048,352]{1,2,0:T(8,128)(2,1)} %param.18) | copy-start | bytes 4325380
  120.4 1.4 copy-start.6
  125.1 41.3 %all-to-all-start.1 = ((bf16[8,48,2048]{2,1,0:T(8,128)(2,1)}), bf16[8,48,2048]{2,1,0:T(8,128)(2,1)S(1)}, u32[]{:S(2)}, u32[]{:S(2)}) async-start(bf16[8,48,2048]{2,1,0:T(8,128)(2,1)} %convolution_convert_fusion), calls=%async_computation.1 | async-start | bytes 3145728 | tf_op jit(solution)/shard_map/all_to_all | solution.py:156
  166.4 2.4 %copy-start.1 = (bf16[512,1024]{1,0:T(8,128)(2,1)S(1)}, bf16[512,1024]{1,0:T(8,128)(2,1)}, u32[]{:S(2)}) copy-start(bf16[512,1024]{1,0:T(8,128)(2,1)} %all-gather.3.cloned.1.call-done) | copy-start | bytes 3145732
  167.3 5.1 %collective-permute-start.2 = (bf16[32,2048]{1,0:T(8,128)(2,1)S(1)}, bf16[32,2048]{1,0:T(8,128)(2,1)S(1)}, u32[]{:S(2)}, u32[]{:S(2)}) collective-permute-start(bf16[32,2048]{1,0:T(8,128)(2,1)S(1)} %select_convert_fusion), channel_id=1, source_target_pairs={{0,1},{1,0},{2,3},{3,2},{4,5},{5,4},{6,7},{7,6},{8,9},{9,8},{10,11... | collective-permute-start | bytes 393224 | tf_op jit(solution)/shard_map/ppermute | solution.py:46
Sparse Core Ops, SparseCore 0:
  10.2 24.8 all-gather.2
  36.6 28.7 all-gather.4
where the time goes:
time: 180 us
  waiting for transfers between devices  96.1 us (53%)
  blocking collectives  41 us (23%)
  between operations  14.9 us (8%)
  matrix products  11.2 us (6%)
  starting transfers between devices  8.24 us (5%)
  local copies, waits for them, and re-layouts  4.62 us (3%)
  other arithmetic  3.95 us (2%)
    all_to_all x1, blocking collectives, local(): lax.all_to_all(send_rows, 'ctx', split_axis=0, concat_axis=0, tiled=True)  41 us
    all_to_all x1, waiting for transfers between devices, local(): lax.all_to_all(produced.astype(jnp.bfloat16), 'ctx', split_axis=0, concat...  35.8 us
    all_gather x1, waiting for transfers between devices, local(): lax.all_gather(out_weight, 'ctx', axis=0, tiled=True)  27.7 us
    all_gather x1, waiting for transfers between devices, local(): kv_all = lax.all_gather(kv_here, 'ctx', axis=0, tiled=True)  22.2 us
    ppermute x3, waiting for transfers between devices, exp_swap(): return lax.ppermute(x, 'exp', perm=[(0, 1), (1, 0)])  9.58 us
    ppermute x3, starting transfers between devices, exp_swap(): return lax.ppermute(x, 'exp', perm=[(0, 1), (1, 0)])  4.58 us
  transfers between devices with their start and end apart: 6, of which 6 were waited for; matrix products, arithmetic and copies ran while one was open for 5% of the time, Pallas kernels for 0%

commit v1 on v0

--- a/solution.py
+++ b/solution.py
@@ -8,6 +8,31 @@
 TOP = 4
 EPS = 1e-06
 NEG = -1e30
+
+
+def laid_out(blocks, dim):
+    shape = list(blocks.shape[1:])
+    shape[dim] *= blocks.shape[0]
+    return jnp.moveaxis(blocks, 0, dim).reshape(shape)
+
+
+def on_each_block(value, axis, dim, apply, out_dim):
+    size, mine, rows = (lax.axis_size(axis), lax.axis_index(axis), value.shape[dim])
+    right = [(i, (i + 1) % size) for i in range(size)]
+    left = [(i, (i - 1) % size) for i in range(size)]
+    halfway = size // 2
+    blocks = {}
+    from_left = from_right = value
+    for step in range(halfway + 1):
+        next_left = lax.ppermute(from_left, axis, right) if step < halfway else None
+        next_right = lax.ppermute(from_right, axis, left) if step < size - halfway - 1 else None
+        blocks[-step] = apply(from_left, (mine - step) % size * rows)
+        if 0 < step < size - halfway:
+            blocks[step] = apply(from_right, (mine + step) % size * rows)
+        from_left, from_right = (next_left, next_right)
+    blocks = jnp.stack([blocks[k] for k in sorted(blocks)])
+    blocks = blocks[(jnp.arange(size) - mine + halfway) % size]
+    return laid_out(blocks, out_dim)
 
 
 def row_positions(row_ids, half_block, n_groups):
@@ -129,11 +154,14 @@
     run_max, run_sum, run_out, kept_keys, kept_values = inner_state + (kept_keys, kept_values)
     mixed = (run_out / run_sum[:, :, None]).astype(jnp.bfloat16)
     mixed = jnp.transpose(mixed, (1, 0, 2)).reshape(tok_here, feat_width)
-    out_parts = jnp.einsum(
-        "tc,oc->to",
-        mixed,
-        lax.all_gather(out_weight, "ctx", axis=0, tiled=True),
-        preferred_element_type=jnp.float32,
+    out_parts = on_each_block(
+        out_weight,
+        "ctx",
+        0,
+        lambda part, offset: jnp.einsum(
+            "tc,oc->to", mixed, part, preferred_element_type=jnp.float32
+        ),
+        1,
     )
     head_total = exp_reduce_rows(out_parts)
     stream = (residual[0].astype(jnp.float32) + head_total).astype(jnp.bfloat16)

time: 180 us -> 170 us (0.944)
  waiting for transfers between devices: 96.1 us -> 68.5 us
  starting transfers between devices: 8.24 us -> 20 us
  matrix products: 11.2 us -> 14.3 us
    all_gather x1 -> x0, waiting for transfers between devices: 27.7 us -> none  [local(): lax.all_gather(out_weight, 'ctx', axis=0, tiled=True)]
    ppermute x0 -> x7, waiting for transfers between devices: none -> 22.7 us  [the longest x4 21.1 us: on_each_block(): next_left = lax.ppermute(from_left, axis, right) if step < halfway else None]
    all_gather x1, waiting for transfers between devices: 22.2 us -> 0.02 us  [local(): kv_all = lax.all_gather(kv_here, 'ctx', axis=0, tiled=True)]
    ppermute x0 -> x7, starting transfers between devices: none -> 12.1 us  [the longest x3 11.6 us: on_each_block(): lax.ppermute(from_right, axis, left)]
    dot_general x1 -> x8, matrix products: 2.33 us -> 5.39 us  [local(): jnp.einsum('tc,oc->to', mixed, part, preferred_element_type=jnp.float32)]
  transfers between devices with their start and end apart: 6 -> 12, of which waited for: 6 -> 10; matrix products, arithmetic and copies ran while one was open for 5% -> 8% of each run, Pallas kernels for 0% -> 0%
where the time goes in v1:
time: 170 us; the launch traced here: 169 us
  waiting for transfers between devices  68.5 us (40%)
  blocking collectives  42.5 us (25%)
  starting transfers between devices  20 us (12%)
  between operations  15 us (9%)
  matrix products  14.3 us (8%)
  local copies, waits for them, and re-layouts  5.25 us (3%)
  other arithmetic  3.99 us (2%)
    all_to_all x1, blocking collectives, local(): lax.all_to_all(send_rows, 'ctx', split_axis=0, concat_axis=0, tiled=True)  42.5 us
    all_to_all x1, waiting for transfers between devices, local(): lax.all_to_all(produced.astype(jnp.bfloat16), 'ctx', split_axis=0, concat...  35.8 us
    ppermute x4, waiting for transfers between devices, on_each_block(): next_left = lax.ppermute(from_left, axis, right) if step < halfway else None  21.1 us
    ppermute x3, starting transfers between devices, on_each_block(): lax.ppermute(from_right, axis, left)  11.6 us
    ppermute x3, waiting for transfers between devices, exp_swap(): return lax.ppermute(x, 'exp', perm=[(0, 1), (1, 0)])  9.95 us
    dot_general x8, matrix products, local(): jnp.einsum('tc,oc->to', mixed, part, preferred_element_type=jnp.float32)  5.39 us
    ppermute x3, starting transfers between devices, exp_swap(): return lax.ppermute(x, 'exp', perm=[(0, 1), (1, 0)])  4.22 us
    all_to_all x1, starting transfers between devices, local(): lax.all_to_all(produced.astype(jnp.bfloat16), 'ctx', split_axis=0, concat...  3.58 us
  transfers between devices with their start and end apart: 12, of which 10 were waited for; matrix products, arithmetic and copies ran while one was open for 8% of the time, Pallas kernels for 0%

profile of v1, /device:TPU:0, one launch (start us, length us, event | category | flops | bytes accessed | tf_op | source)
XLA Modules:
  0.0 169.5 jit_solution(3915362880297165946)
XLA Ops:
  7.2 1.6 pad_maximum_fusion
  8.9 0.5 collective-permute-start
  9.4 4.1 %collective-permute-start.4 = (bf16[256,512]{1,0:T(8,128)(2,1)}, bf16[256,512]{1,0:T(8,128)(2,1)S(1)}, u32[]{:S(2)}, u32[]{:S(2)}) collective-permute-start(bf16[256,512]{1,0:T(8,128)(2,1)} %param.16), channel_id=1, source_target_pairs={{0,14},{2,0},{4,2},{6,4},{8,6},{10,8},{12,10},{14,12},{1,15},{3,1}... | collective-permute-start | bytes 786440 | tf_op jit(solution)/shard_map/ppermute | solution.py:28
  14.1 0.8 copy.53
  15.1 0.6 reduce-window.6
  15.7 0.2 slice_reduce_fusion
  15.9 2.0 %collective-permute-done = bf16[256,512]{1,0:T(8,128)(2,1)S(1)} collective-permute-done((bf16[256,512]{1,0:T(8,128)(2,1)}, bf16[256,512]{1,0:T(8,128)(2,1)S(1)}, u32[]{:S(2)}, u32[]{:S(2)}) %collective-permute-start) | collective-permute-done | bytes 262176 | tf_op jit(solution)/shard_map/ppermute | solution.py:27
  18.1 0.3 collective-permute-done.4
  18.5 3.7 %collective-permute-start.5 = (bf16[256,512]{1,0:T(8,128)(2,1)S(1)}, bf16[256,512]{1,0:T(8,128)(2,1)}, u32[]{:S(2)}, u32[]{:S(2)}) collective-permute-start(bf16[256,512]{1,0:T(8,128)(2,1)S(1)} %collective-permute-done.4), channel_id=1, source_target_pairs={{0,14},{2,0},{4,2},{6,4},{8,6},{10,8},{12,10},{14,12},{1,15},{3,1}... | collective-permute-start | bytes 786440 | tf_op jit(solution)/shard_map/ppermute | solution.py:28
  22.2 4.6 %collective-permute-done.1 = bf16[256,512]{1,0:T(8,128)(2,1)S(1)} collective-permute-done((bf16[256,512]{1,0:T(8,128)(2,1)S(1)}, bf16[256,512]{1,0:T(8,128)(2,1)S(1)}, u32[]{:S(2)}, u32[]{:S(2)}) %collective-permute-start.1) | collective-permute-done | bytes 262176 | tf_op jit(solution)/shard_map/ppermute | solution.py:27
  26.9 0.9 reshape_squeeze.4
  27.8 1.2 collective-permute-done.5
  29.1 3.8 %collective-permute-start.6 = (bf16[256,512]{1,0:T(8,128)(2,1)}, bf16[256,512]{1,0:T(8,128)(2,1)}, u32[]{:S(2)}, u32[]{:S(2)}) collective-permute-start(bf16[256,512]{1,0:T(8,128)(2,1)} %collective-permute-done.5), channel_id=1, source_target_pairs={{0,14},{2,0},{4,2},{6,4},{8,6},{10,8},{12,10},{14,12},{1,15},{3,1}... | collective-permute-start | bytes 786440 | tf_op jit(solution)/shard_map/ppermute | solution.py:28
  32.9 6.8 %collective-permute-done.2 = bf16[256,512]{1,0:T(8,128)(2,1)} collective-permute-done((bf16[256,512]{1,0:T(8,128)(2,1)S(1)}, bf16[256,512]{1,0:T(8,128)(2,1)}, u32[]{:S(2)}, u32[]{:S(2)}) %collective-permute-start.2) | collective-permute-done | bytes 262176 | tf_op jit(solution)/shard_map/ppermute | solution.py:27
  39.7 1.3 fusion.95
  41.0 0.2 copy.60
  41.2 0.3 fusion.96
  41.5 0.2 copy.61
  41.7 0.2 fusion.26
  42.0 0.3 fusion.15
  42.3 7.8 %collective-permute-done.3 = bf16[256,512]{1,0:T(8,128)(2,1)} collective-permute-done((bf16[256,512]{1,0:T(8,128)(2,1)}, bf16[256,512]{1,0:T(8,128)(2,1)}, u32[]{:S(2)}, u32[]{:S(2)}) %collective-permute-start.3) | collective-permute-done | bytes 262176 | tf_op jit(solution)/shard_map/ppermute | solution.py:27
  50.1 1.2 fusion.23
  51.3 1.2 fusion.22
  52.5 0.2 fusion.21
  52.7 0.2 fusion.20
  53.1 0.2 fusion.18
  53.3 1.2 fusion.17
  54.4 1.1 fusion.16
  55.6 0.6 gather_fusion
  56.3 1.1 collective-permute-start.7
  57.5 3.8 %collective-permute-done.7 = bf16[32,2048]{1,0:T(8,128)(2,1)S(1)} collective-permute-done((bf16[32,2048]{1,0:T(8,128)(2,1)S(1)}, bf16[32,2048]{1,0:T(8,128)(2,1)S(1)}, u32[]{:S(2)}, u32[]{:S(2)}) %collective-permute-start.7) | collective-permute-done | bytes 131104 | tf_op jit(solution)/shard_map/ppermute | solution.py:71
  61.6 1.1 collective-permute-start.8
  63.0 3.7 %collective-permute-done.8 = bf16[32,2048]{1,0:T(8,128)(2,1)S(1)} collective-permute-done((bf16[32,2048]{1,0:T(8,128)(2,1)S(1)}, bf16[32,2048]{1,0:T(8,128)(2,1)S(1)}, u32[]{:S(2)}, u32[]{:S(2)}) %collective-permute-start.8) | collective-permute-done | bytes 131104 | tf_op jit(solution)/shard_map/ppermute | solution.py:71
  66.6 0.6 convolution_convert_fusion.1
  67.2 42.5 %all_to_all.10 = bf16[8,48,2048]{2,1,0:T(8,128)(2,1)S(1)} all-to-all(bf16[8,48,2048]{2,1,0:T(8,128)(2,1)S(1)} %bitcast.135), channel_id=1, replica_groups=mesh['req'=2,'ctx'=8,'exp'=2] {'ctx'}, dimensions={0} | all-to-all | bytes 3145728 | tf_op jit(solution)/shard_map/all_to_all | solution.py:178
  109.7 0.9 fusion.3
  110.6 0.4 copy-done.11
  111.1 0.9 fusion.10
  112.0 0.2 copy.57
  112.2 2.2 %convolution_convert_fusion = bf16[8,48,2048]{2,1,0:T(8,128)(2,1)} fusion(bf16[8,48,352]{2,1,0:T(8,128)(2,1)S(1)} %bitcast.141, bf16[1,352,2048]{2,1,0:T(8,128)(2,1)S(1)} %copy-done), kind=kOutput, calls=%fused_computation.1 | convolution fusion | flops 554434560 | bytes 3284992 | tf_op jit(solution)/shard_map/dot_general | solution.py:67
  114.4 3.6 %all-to-all-start.1 = ((bf16[8,48,2048]{2,1,0:T(8,128)(2,1)}), bf16[8,48,2048]{2,1,0:T(8,128)(2,1)S(1)}, u32[]{:S(2)}, u32[]{:S(2)}) async-start(bf16[8,48,2048]{2,1,0:T(8,128)(2,1)} %convolution_convert_fusion), calls=%async_computation.1 | async-start | bytes 3145728 | tf_op jit(solution)/shard_map/all_to_all | solution.py:184
  118.0 1.9 %fusion.25 = bf16[1,64,512]{2,1,0:T(8,128)(2,1)} fusion(s32[512]{0:T(512)S(1)} %fusion.78, s32[64]{0:T(128)S(1)} %iota_add_fusion, bf16[512,1024]{1,0:T(8,128)(2,1)} %all-gather.2.cloned.1.call-done), kind=kOutput, calls=%fused_computation.36 | convolution fusion | flops 33619968 | bytes 592128 | tf_op jit(solution)/shard_map/dot_general | solution.py:134
  119.9 35.8 %all-to-all-done.1 = bf16[8,48,2048]{2,1,0:T(8,128)(2,1)S(1)} async-done(((bf16[8,48,2048]{2,1,0:T(8,128)(2,1)}), bf16[8,48,2048]{2,1,0:T(8,128)(2,1)S(1)}, u32[]{:S(2)}, u32[]{:S(2)}) %all-to-all-start.1) | async-done | bytes 1572896 | tf_op jit(solution)/shard_map/all_to_all | solution.py:184
  155.7 0.9 fusion.97
  156.6 2.0 %collective-permute-start.9 = (bf16[32,2048]{1,0:T(8,128)(2,1)S(1)}, bf16[32,2048]{1,0:T(8,128)(2,1)S(1)}, u32[]{:S(2)}, u32[]{:S(2)}) collective-permute-start(bf16[32,2048]{1,0:T(8,128)(2,1)S(1)} %select_convert_fusion), channel_id=1, source_target_pairs={{0,1},{1,0},{2,3},{3,2},{4,5},{5,4},{6,7},{7,6},{8,9},{9,8},{10,11... | collective-permute-start | bytes 393224 | tf_op jit(solution)/shard_map/ppermute | solution.py:71
  158.6 0.9 fusion.24
  159.5 2.4 %collective-permute-done.9 = bf16[32,2048]{1,0:T(8,128)(2,1)S(1)} collective-permute-done((bf16[32,2048]{1,0:T(8,128)(2,1)S(1)}, bf16[32,2048]{1,0:T(8,128)(2,1)S(1)}, u32[]{:S(2)}, u32[]{:S(2)}) %collective-permute-start.9) | collective-permute-done | bytes 131104 | tf_op jit(solution)/shard_map/ppermute | solution.py:71
  161.9 0.7 fusion.46
  (57 shorter events, 1.6 us)
Async XLA Ops:
  7.2 105.1 %copy-start = (bf16[1,352,2048]{2,1,0:T(8,128)(2,1)S(1)}, bf16[1,352,2048]{2,1,0:T(8,128)(2,1)}, u32[]{:S(2)}) copy-start(bf16[1,352,2048]{2,1,0:T(8,128)(2,1)} %param.20) | copy-start | bytes 4325380
  7.2 32.5 %all-gather.2.cloned.1.call-start = ((), (), s32[]{:S(2)}) async-start(), calls=%async_computation.2 | async-start | bytes 1179648 | tf_op jit(solution)/shard_map/all_gather | solution.py:127
  8.9 9.0 %collective-permute-start = (bf16[256,512]{1,0:T(8,128)(2,1)}, bf16[256,512]{1,0:T(8,128)(2,1)S(1)}, u32[]{:S(2)}, u32[]{:S(2)}) collective-permute-start(bf16[256,512]{1,0:T(8,128)(2,1)} %param.16), channel_id=1, source_target_pairs={{0,2},{2,4},{4,6},{6,8},{8,10},{10,12},{12,14},{14,0},{1,3},{3,5},... | collective-permute-start | bytes 786440 | tf_op jit(solution)/shard_map/ppermute | solution.py:27
  9.4 9.1 %collective-permute-start.4 = (bf16[256,512]{1,0:T(8,128)(2,1)}, bf16[256,512]{1,0:T(8,128)(2,1)S(1)}, u32[]{:S(2)}, u32[]{:S(2)}) collective-permute-start(bf16[256,512]{1,0:T(8,128)(2,1)} %param.16), channel_id=1, source_target_pairs={{0,14},{2,0},{4,2},{6,4},{8,6},{10,8},{12,10},{14,12},{1,15},{3,1}... | collective-permute-start | bytes 786440 | tf_op jit(solution)/shard_map/ppermute | solution.py:28
  17.9 21.8 %copy-start.3 = (bf16[256,512]{1,0:T(8,128)(2,1)}, bf16[256,512]{1,0:T(8,128)(2,1)S(1)}, u32[]{:S(2)}) copy-start(bf16[256,512]{1,0:T(8,128)(2,1)S(1)} %collective-permute-done) | copy-start | bytes 786436
  17.9 8.9 %collective-permute-start.1 = (bf16[256,512]{1,0:T(8,128)(2,1)S(1)}, bf16[256,512]{1,0:T(8,128)(2,1)S(1)}, u32[]{:S(2)}, u32[]{:S(2)}) collective-permute-start(bf16[256,512]{1,0:T(8,128)(2,1)S(1)} %collective-permute-done), channel_id=1, source_target_pairs={{0,2},{2,4},{4,6},{6,8},{8,10},{10,12},{12,14},{14,0},{1,3},{3,5},... | collective-permute-start | bytes 786440 | tf_op jit(solution)/shard_map/ppermute | solution.py:27
  18.5 10.6 %collective-permute-start.5 = (bf16[256,512]{1,0:T(8,128)(2,1)S(1)}, bf16[256,512]{1,0:T(8,128)(2,1)}, u32[]{:S(2)}, u32[]{:S(2)}) collective-permute-start(bf16[256,512]{1,0:T(8,128)(2,1)S(1)} %collective-permute-done.4), channel_id=1, source_target_pairs={{0,14},{2,0},{4,2},{6,4},{8,6},{10,8},{12,10},{14,12},{1,15},{3,1}... | collective-permute-start | bytes 786440 | tf_op jit(solution)/shard_map/ppermute | solution.py:28
  26.7 12.9 %copy-start.5 = (bf16[256,512]{1,0:T(8,128)(2,1)}, bf16[256,512]{1,0:T(8,128)(2,1)S(1)}, u32[]{:S(2)}) copy-start(bf16[256,512]{1,0:T(8,128)(2,1)S(1)} %collective-permute-done.1) | copy-start | bytes 786436
  26.7 12.9 %collective-permute-start.2 = (bf16[256,512]{1,0:T(8,128)(2,1)S(1)}, bf16[256,512]{1,0:T(8,128)(2,1)}, u32[]{:S(2)}, u32[]{:S(2)}) collective-permute-start(bf16[256,512]{1,0:T(8,128)(2,1)S(1)} %collective-permute-done.1), channel_id=1, source_target_pairs={{0,2},{2,4},{4,6},{6,8},{8,10},{10,12},{12,14},{14,0},{1,3},{3,5},... | collective-permute-start | bytes 786440 | tf_op jit(solution)/shard_map/ppermute | solution.py:27
  29.1 25.4 %collective-permute-start.6 = (bf16[256,512]{1,0:T(8,128)(2,1)}, bf16[256,512]{1,0:T(8,128)(2,1)}, u32[]{:S(2)}, u32[]{:S(2)}) collective-permute-start(bf16[256,512]{1,0:T(8,128)(2,1)} %collective-permute-done.5), channel_id=1, source_target_pairs={{0,14},{2,0},{4,2},{6,4},{8,6},{10,8},{12,10},{14,12},{1,15},{3,1}... | collective-permute-start | bytes 786440 | tf_op jit(solution)/shard_map/ppermute | solution.py:28
  39.7 10.5 %collective-permute-start.3 = (bf16[256,512]{1,0:T(8,128)(2,1)}, bf16[256,512]{1,0:T(8,128)(2,1)}, u32[]{:S(2)}, u32[]{:S(2)}) collective-permute-start(bf16[256,512]{1,0:T(8,128)(2,1)} %collective-permute-done.2), channel_id=1, source_target_pairs={{0,2},{2,4},{4,6},{6,8},{8,10},{10,12},{12,14},{14,0},{1,3},{3,5},... | collective-permute-start | bytes 786440 | tf_op jit(solution)/shard_map/ppermute | solution.py:27
  41.7 10.7 %copy-start.6 = (bf16[256,512]{1,0:T(8,128)(2,1)S(1)}, bf16[256,512]{1,0:T(8,128)(2,1)}, u32[]{:S(2)}) copy-start(bf16[256,512]{1,0:T(8,128)(2,1)} %copy-done.5) | copy-start | bytes 786436
  41.7 10.9 %copy-start.4 = (bf16[256,512]{1,0:T(8,128)(2,1)S(1)}, bf16[256,512]{1,0:T(8,128)(2,1)}, u32[]{:S(2)}) copy-start(bf16[256,512]{1,0:T(8,128)(2,1)} %copy-done.3) | copy-start | bytes 786436
  42.0 10.9 %copy-start.2 = (bf16[256,512]{1,0:T(8,128)(2,1)S(1)}, bf16[256,512]{1,0:T(8,128)(2,1)}, u32[]{:S(2)}) copy-start(bf16[256,512]{1,0:T(8,128)(2,1)} %param.16) | copy-start | bytes 786436
  55.6 5.7 %copy-start.7 = (bf16[1,32,2048]{2,1,0:T(8,128)(2,1)S(1)}, bf16[1,32,2048]{2,1,0:T(8,128)(2,1)}, u32[]{:S(2)}) copy-start(bf16[1,32,2048]{2,1,0:T(8,128)(2,1)} %param.15) | copy-start | bytes 393220
  56.2 5.3 %copy-start.8 = (f32[2048]{0:T(1024)S(1)}, f32[2048]{0:T(1024)}, u32[]{:S(2)}) copy-start(f32[2048]{0:T(1024)} %param.17) | copy-start | bytes 24580
  56.2 6.6 %copy-start.9 = (f32[1,64,4]{1,2,0:T(4,128)S(1)}, f32[1,64,4]{1,2,0:T(4,128)}, u32[]{:S(2)}) copy-start(f32[1,64,4]{1,2,0:T(4,128)} %param.22) | copy-start | bytes 3076
  56.3 5.0 %collective-permute-start.7 = (bf16[32,2048]{1,0:T(8,128)(2,1)S(1)}, bf16[32,2048]{1,0:T(8,128)(2,1)S(1)}, u32[]{:S(2)}, u32[]{:S(2)}) collective-permute-start(bf16[32,2048]{1,0:T(8,128)(2,1)S(1)} %bitcast.144), channel_id=1, source_target_pairs={{0,1},{1,0},{2,3},{3,2},{4,5},{5,4},{6,7},{7,6},{8,9},{9,8},{10,11... | collective-permute-start | bytes 393224 | tf_op jit(solution)/shard_map/ppermute | solution.py:71
  61.6 5.0 %collective-permute-start.8 = (bf16[32,2048]{1,0:T(8,128)(2,1)S(1)}, bf16[32,2048]{1,0:T(8,128)(2,1)S(1)}, u32[]{:S(2)}, u32[]{:S(2)}) collective-permute-start(bf16[32,2048]{1,0:T(8,128)(2,1)S(1)} %fusion.30), channel_id=1, source_target_pairs={{0,1},{1,0},{2,3},{3,2},{4,5},{5,4},{6,7},{7,6},{8,9},{9,8},{10,11... | collective-permute-start | bytes 393224 | tf_op jit(solution)/shard_map/ppermute | solution.py:71
  67.2 42.5 %copy-start.10 = (bf16[1,2048,352]{1,2,0:T(8,128)(2,1)S(1)}, bf16[1,2048,352]{1,2,0:T(8,128)(2,1)}, u32[]{:S(2)}) copy-start(bf16[1,2048,352]{1,2,0:T(8,128)(2,1)} %param.18) | copy-start | bytes 4325380
  109.7 1.4 copy-start.11
  114.4 41.3 %all-to-all-start.1 = ((bf16[8,48,2048]{2,1,0:T(8,128)(2,1)}), bf16[8,48,2048]{2,1,0:T(8,128)(2,1)S(1)}, u32[]{:S(2)}, u32[]{:S(2)}) async-start(bf16[8,48,2048]{2,1,0:T(8,128)(2,1)} %convolution_convert_fusion), calls=%async_computation.1 | async-start | bytes 3145728 | tf_op jit(solution)/shard_map/all_to_all | solution.py:184
  155.7 2.9 %copy-start.1 = (bf16[512,1024]{1,0:T(8,128)(2,1)S(1)}, bf16[512,1024]{1,0:T(8,128)(2,1)}, u32[]{:S(2)}) copy-start(bf16[512,1024]{1,0:T(8,128)(2,1)} %all-gather.2.cloned.1.call-done) | copy-start | bytes 3145732
  156.6 5.3 %collective-permute-start.9 = (bf16[32,2048]{1,0:T(8,128)(2,1)S(1)}, bf16[32,2048]{1,0:T(8,128)(2,1)S(1)}, u32[]{:S(2)}, u32[]{:S(2)}) collective-permute-start(bf16[32,2048]{1,0:T(8,128)(2,1)S(1)} %select_convert_fusion), channel_id=1, source_target_pairs={{0,1},{1,0},{2,3},{3,2},{4,5},{5,4},{6,7},{7,6},{8,9},{9,8},{10,11... | collective-permute-start | bytes 393224 | tf_op jit(solution)/shard_map/ppermute | solution.py:71
Sparse Core Ops, SparseCore 0:
  10.2 29.0 all-gather.1
